TPU v7x, 32 devices: a whole 2x2x4 slice. The times are simulated.
32 devices in a mesh: groups: 2 (over y), lat: 8 (over z, x), seed: 2 (over core).
Axes of the slice: x: 2, y: 2, z: 4, core: 2. Of those that a mesh axis runs over, the one named last changes fastest.
Arguments:
- activations: bfloat16 [512, 2048], P(('groups', 'seed'), 'lat'), parts along dimension 0, may hold values from -6 to 6
- bag_rows: int32 [4, 256], P(('groups', 'seed')), parts along dimension 0, may hold values from 0 to 255
- keep_cols: int32 [4, 2048], P(('groups', 'seed')), parts along dimension 0, may hold values 0 or 1
- enc_weight: bfloat16 [4, 16384, 2048], P(('groups', 'seed'), 'lat'), parts along dimension 0, may hold values from -0.125 to 0.125
- enc_bias: float32 [4, 16384], P(('groups', 'seed'), 'lat'), parts along dimension 0, may hold values from -3 to 3
- dec_weight: bfloat16 [4, 16384, 2048], P(('groups', 'seed'), 'lat'), parts along dimension 0, may hold values from -0.0625 to 0.0625
- dec_bias: float32 [4, 2048], P(('groups', 'seed')), parts along dimension 0, may hold values from -3 to 3
- first_moment: bfloat16 [4, 16384, 2048], P(('groups', 'seed'), 'lat'), parts along dimension 0, may hold values from -0.3125 to 0.3125
- second_moment: bfloat16 [4, 16384, 2048], P(('groups', 'seed'), 'lat'), parts along dimension 0, may hold values from 9.9658966e-05 to 0.0099487305
Outputs:
- new_weight: bfloat16 [4, 16384, 2048], P(('groups', 'seed'), 'lat'), parts along dimension 0
- new_first: bfloat16 [4, 16384, 2048], P(('groups', 'seed'), 'lat'), parts along dimension 0
- new_second: bfloat16 [4, 16384, 2048], P(('groups', 'seed'), 'lat'), parts along dimension 0
There are 2 independent parts, one for each index of `groups`. A program takes and returns all parts, laid end to end along the dimension named above; each array names one. Nothing has to cross between parts.
All inputs are finite; a program needn't handle non-finite values. No bound on the sum of `keep_cols` on one device may be relied on, other than what follows from the above.
Results may differ from a plain program's by a relative error of at most 0.012.
The roundings to bfloat16 on the way count: a program that leaves them out, or rounds other values in their place, can miss the bound.
Values may be sent and summed in bfloat16 or wider, within the bound.
No kernel may reach another device: no remote copies, remote signals or barrier semaphores. Data moves between devices by JAX's collectives and lax.ppermute only.
A program may use at most 128 MiB of HBM per device.

v0:
```python
import jax
import jax.numpy as jnp
from jax import lax
from jax.sharding import PartitionSpec as P

sparsity = 0.2
beta_one = 0.9
beta_two = 0.95
corr_one = 1.0 - 0.9**10
corr_two = 1.0 - 0.95**10
adam_eps = 1e-08
rate_step = 0.001
decay_rate = 0.1


def local(
    activations,
    bag_rows,
    keep_cols,
    enc_weight,
    enc_bias,
    dec_weight,
    dec_bias,
    first_moment,
    second_moment,
):
    half_rows = lax.all_gather(activations, "lat", axis=1, tiled=True)
    gathered = lax.all_gather(half_rows, "seed", axis=0, tiled=True)
    row_order = bag_rows[0]
    sample = jnp.take(gathered, row_order, axis=0)
    weight_in = enc_weight[0]
    decoder = dec_weight[0]
    bias_dec = dec_bias[0]
    keep = keep_cols[0].astype(jnp.float32)
    centered = (sample.astype(jnp.float32) - bias_dec).astype(jnp.bfloat16)
    pre_t = lax.dot_general(
        weight_in, centered, (((1,), (1,)), ((), ())), preferred_element_type=jnp.float32
    )
    pre_t = pre_t + enc_bias[0][:, None]
    latent_t = jnp.maximum(pre_t, 0.0).astype(jnp.bfloat16)
    partial_sum = lax.dot_general(
        latent_t, decoder, (((0,), (0,)), ((), ())), preferred_element_type=jnp.float32
    )
    total = lax.psum(partial_sum, "lat")
    error = ((total + bias_dec - sample.astype(jnp.float32)) * keep).astype(jnp.bfloat16)
    back_t = lax.dot_general(
        decoder, error, (((1,), (1,)), ((), ())), preferred_element_type=jnp.float32
    )
    row_norm = jnp.sqrt(jnp.sum(jnp.square(decoder.astype(jnp.float32)), axis=1) + 1e-06)
    token_total = sample.shape[0]
    d_pre_t = (
        jnp.where(pre_t > 0, 2.0 * back_t + sparsity * row_norm[:, None], 0.0) / token_total
    ).astype(jnp.bfloat16)
    grad = jnp.dot(d_pre_t, centered, preferred_element_type=jnp.float32)
    moment_one = beta_one * first_moment[0].astype(jnp.float32) + (1.0 - beta_one) * grad
    moment_two = beta_two * second_moment[0].astype(jnp.float32) + (1.0 - beta_two) * grad * grad
    direction = moment_one / corr_one / (jnp.sqrt(moment_two / corr_two) + adam_eps)
    old = weight_in.astype(jnp.float32)
    updated = (old - rate_step * (direction + decay_rate * old)).astype(jnp.bfloat16)
    return (
        updated[None],
        moment_one.astype(jnp.bfloat16)[None],
        moment_two.astype(jnp.bfloat16)[None],
    )


def solution(mesh):
    return jax.shard_map(
        local,
        mesh=mesh,
        in_specs=(
            P(("groups", "seed"), "lat"),
            P(("groups", "seed"), None),
            P(("groups", "seed"), None),
            P(("groups", "seed"), "lat", None),
            P(("groups", "seed"), "lat"),
            P(("groups", "seed"), "lat", None),
            P(("groups", "seed"), None),
            P(("groups", "seed"), "lat", None),
            P(("groups", "seed"), "lat", None),
        ),
        out_specs=(
            P(("groups", "seed"), "lat", None),
            P(("groups", "seed"), "lat", None),
            P(("groups", "seed"), "lat", None),
        ),
        check_vma=False,
    )
```

profile of v0, /device:TPU:0, one launch (start us, length us, event | category | flops | bytes accessed | tf_op | source)
XLA Modules:
  0.0 222.0 jit_solution(16715430085450274316)
XLA Ops:
  7.2 0.0 copy-start
  7.2 0.0 copy-start.2
  7.2 0.0 all-gather.2.cloned.1.call-start
  7.2 35.4 %all_gather.6 = bf16[128,2048]{1,0:T(8,128)(2,1)} all-gather(bf16[128,256]{1,0:T(8,128)(2,1)} %param.9), channel_id=1, replica_groups=mesh['groups'=2,'lat'=8,'seed'=2] {'lat'}, dimensions={1}, use_global_device_ids=true | all-gather | bytes 589824 | tf_op jit(solution)/shard_map/all_gather | solution.py:27
  42.6 0.0 all-gather.2.cloned.1.call-update
  42.7 0.0 all-reduce.2.cloned.1.call-start
  42.7 0.7 compare_select_fusion
  43.4 0.7 compare_and_fusion
  44.1 8.8 %all-gather.2.cloned.1.call-done = bf16[256,2048]{1,0:T(8,128)(2,1)} async-done(((bf16[128,2048]{1,0:T(8,128)(2,1)}), bf16[256,2048]{1,0:T(8,128)(2,1)}) %all-gather.2.cloned.1.call-update) | async-done | bytes 1048592 | tf_op jit(solution)/shard_map/all_gather | solution.py:28
  52.9 3.7 %gather_fusion = bf16[256,2048]{1,0:T(8,128)(2,1)S(1)} fusion(bf16[256,2048]{1,0:T(8,128)(2,1)} %all-gather.2.cloned.1.call-done, s32[1024]{0:T(1024)S(1)} %pad_clamp_fusion), kind=kCustom, calls=%fused_computation | custom fusion | bytes 2098176 | tf_op jit(solution)/shard_map/jit(_take)/gather | solution.py:30
  56.6 0.0 copy-done
  56.6 0.0 copy-done.2
  56.7 5.8 %fusion.27 = f32[256,2048]{1,0:T(8,128)S(1)} fusion(bf16[1,2048,2048]{2,1,0:T(8,128)(2,1)} %param.12, f32[2048]{0:T(1024)S(1)} %bitcast.64, f32[2048]{0:T(1024)S(1)} %bitcast.59, bf16[256,2048]{1,0:T(8,128)(2,1)S(1)} %gather_fusion, pred[256]{0:T(512)(128)(4,1)S(1)} %compare_and_fusion), kind=kOutput, calls=%fused_computation.27 | convolution fusion | flops 2150105088 | bytes 11550976 | tf_op jit(solution)/shard_map/dot_general | solution.py:36
  62.4 0.0 copy-start.1
  62.5 7.0 %fusion.10 = f32[256,2048]{1,0:T(8,128)} fusion(bf16[1,2048,2048]{2,1,0:T(8,128)(2,1)} %param.14, f32[256,2048]{1,0:T(8,128)S(1)} %fusion.27), kind=kOutput, calls=%fused_computation.16 | convolution fusion | flops 2148532224 | bytes 12582912 | tf_op jit(solution)/shard_map/dot_general | solution.py:41
  69.5 0.0 all-reduce.2.cloned.1.call-update
  69.5 0.0 copy-done.1
  69.5 5.1 %multiply_reduce_fusion = f32[2048]{0:T(1024)S(1)} fusion(bf16[1,2048,2048]{2,1,0:T(8,128)(2,1)} %param.14), kind=kLoop, calls=%fused_computation.9 | loop fusion | flops 12580864 | bytes 8396800 | tf_op jit(solution)/shard_map/reduce_sum | solution.py:49
  74.6 98.0 %all-reduce.2.cloned.1.call-done = f32[256,2048]{1,0:T(8,128)} async-done(((f32[256,2048]{1,0:T(8,128)}), f32[256,2048]{1,0:T(8,128)}) %all-reduce.2.cloned.1.call-update) | async-done | bytes 2097168 | tf_op jit(solution)/shard_map/psum | solution.py:44
  172.7 14.7 %fusion.34 = f32[2048,2048]{1,0:T(8,128)} fusion(bf16[1,2048,2048]{2,1,0:T(8,128)(2,1)} %param.14, f32[256,2048]{1,0:T(8,128)S(1)} %fusion.27, f32[256,2048]{1,0:T(8,128)} %all-reduce.2.cloned.1.call-done, f32[2048]{0:T(1024)S(1)} %sqrt_multiply_fusion, f32[2048]{0:T(1024)S(1)} %bitcast.61, f32[2048]{0:T(1024)S(1)} %bitcast.60, ...), kind=kOutput, calls=%fused_computation.29 | convolution fusion | flops 4303355904 | bytes 30433536 | tf_op jit(solution)/shard_map/dot_general | solution.py:54
  187.3 27.9 %fusion.6 = (bf16[1,2048,2048]{2,1,0:T(8,128)(2,1)}, bf16[1,2048,2048]{2,1,0:T(8,128)(2,1)}, bf16[1,2048,2048]{2,1,0:T(8,128)(2,1)}) fusion(f32[2048,2048]{1,0:T(8,128)} %fusion.34, bf16[1,2048,2048]{2,1,0:T(8,128)(2,1)} %param.17, bf16[1,2048,2048]{2,1,0:T(8,128)(2,1)} %param.16, bf16[1,2048,2048]{2,1,0:T(8,128)(2,1)} %param.12), kind=kLoop, calls=%fused_computation.12 | loop fusion | flops 88080384 | bytes 67108864 | tf_op jit(solution)/shard_map/broadcast_in_dim | solution.py:63
  (3 shorter events, 0.0 us)
Async XLA Ops:
  7.2 49.5 %copy-start = (f32[1,2048]{1,0:T(1,128)S(1)}, f32[1,2048]{1,0:T(1,128)}, u32[]{:S(2)}) copy-start(f32[1,2048]{1,0:T(1,128)} %param.15) | copy-start | bytes 24580
  7.2 49.5 %copy-start.2 = (f32[1,2048]{1,0:T(1,128)S(1)}, f32[1,2048]{1,0:T(1,128)}, u32[]{:S(2)}) copy-start(f32[1,2048]{1,0:T(1,128)} %param.13) | copy-start | bytes 24580
  7.2 45.7 %all-gather.2.cloned.1.call-start = ((), (), s32[]{:S(2)}) async-start(), calls=%async_computation | async-start | bytes 1572864 | tf_op jit(solution)/shard_map/all_gather | solution.py:28
  42.7 130.0 %all-reduce.2.cloned.1.call-start = ((), (), s32[]{:S(2)}) async-start(), calls=%async_computation.1 | async-start | bytes 4194304 | tf_op jit(solution)/shard_map/psum | solution.py:44
  62.4 7.1 %copy-start.1 = (s32[1,2048]{1,0:T(1,128)S(1)}, s32[1,2048]{1,0:T(1,128)}, u32[]{:S(2)}) copy-start(s32[1,2048]{1,0:T(1,128)} %param.11) | copy-start | bytes 24580
Sparse Core Ops, SparseCore 0:
  42.8 10.0 all-gather.1
  69.6 103.0 all-reduce.1
where the time goes:
time: 222 us
  waiting for transfers between devices  107 us (48%)
  blocking collectives  35.4 us (16%)
  other arithmetic  34.3 us (15%)
  matrix products  27.5 us (12%)
  between operations  14.1 us (6%)
  local copies, waits for them, and re-layouts  3.74 us (2%)
    psum x1, waiting for transfers between devices, local(): total = lax.psum(partial_sum, 'lat')  98 us
    all_gather x1, blocking collectives, local(): half_rows = lax.all_gather(activations, 'lat', axis=1, tiled=True)  35.4 us
    broadcast_in_dim x1, other arithmetic, local(): moment_two.astype(jnp.bfloat16)[None]  27.9 us
    dot_general x1, matrix products, local(): grad = jnp.dot(d_pre_t, centered, preferred_element_type=jnp.float32)  14.7 us
    all_gather x1, waiting for transfers between devices, local(): gathered = lax.all_gather(half_rows, 'seed', axis=0, tiled=True)  8.8 us
    dot_general x1, matrix products, local(): lax.dot_general(latent_t, decoder, (((0,), (0,)), ((), ())), preferred_el...  7.04 us
    dot_general x1, matrix products, local(): lax.dot_general(weight_in, centered, (((1,), (1,)), ((), ())), preferred_...  5.77 us
    reduce_sum x1, other arithmetic, local(): jnp.sum(jnp.square(decoder.astype(jnp.float32)), axis=1) + 1e-06  5.08 us
  transfers between devices with their start and end apart: 2, of which 2 were waited for; matrix products, arithmetic and copies ran while one was open for 3% of the time, Pallas kernels for 0%

commit v1 on v0

--- a/solution.py
+++ b/solution.py
@@ -24,7 +24,12 @@
     first_moment,
     second_moment,
 ):
-    half_rows = lax.all_gather(activations, "lat", axis=1, tiled=True)
+    ring = [activations]
+    for hop in range(7):
+        ring.append(lax.ppermute(ring[-1], "lat", [(dev, (dev + 1) % 8) for dev in range(8)]))
+    half_rows = jnp.roll(
+        jnp.concatenate(ring[::-1], axis=1), (lax.axis_index("lat") + 1) * ring[0].shape[1], axis=1
+    )
     gathered = lax.all_gather(half_rows, "seed", axis=0, tiled=True)
     row_order = bag_rows[0]
     sample = jnp.take(gathered, row_order, axis=0)

time: 222 us -> 237 us (1.068)
  waiting for transfers between devices: 107 us -> 151 us
  blocking collectives: 35.4 us -> 0 us
  starting transfers between devices: 0.08 us -> 3.09 us
  local copies, waits for them, and re-layouts: 3.74 us -> 6.36 us
    ppermute x0 -> x7, waiting for transfers between devices: none -> 47.7 us  [local(): lax.ppermute(ring[-1], 'lat', [(dev, (dev + 1) % 8) for dev in range(8)])]
    all_gather x1 -> x0, blocking collectives: 35.4 us -> none  [local(): half_rows = lax.all_gather(activations, 'lat', axis=1, tiled=True)]
    all_gather x1, waiting for transfers between devices: 8.8 us -> 5.33 us  [local(): gathered = lax.all_gather(half_rows, 'seed', axis=0, tiled=True)]
    ppermute x0 -> x7, starting transfers between devices: none -> 3.01 us  [local(): lax.ppermute(ring[-1], 'lat', [(dev, (dev + 1) % 8) for dev in range(8)])]
  transfers between devices with their start and end apart: 2 -> 9, of which waited for: 2 -> 9; matrix products, arithmetic and copies ran while one was open for 3% -> 3% of each run, Pallas kernels for 0% -> 0%
where the time goes in v1:
time: 237 us
  waiting for transfers between devices  151 us (64%)
  other arithmetic  34.3 us (14%)
  matrix products  27.5 us (12%)
  between operations  14.2 us (6%)
  local copies, waits for them, and re-layouts  6.36 us (3%)
  starting transfers between devices  3.09 us (1%)
    psum x1, waiting for transfers between devices, local(): total = lax.psum(partial_sum, 'lat')  98 us
    ppermute x7, waiting for transfers between devices, local(): lax.ppermute(ring[-1], 'lat', [(dev, (dev + 1) % 8) for dev in range(8)])  47.7 us
    broadcast_in_dim x1, other arithmetic, local(): moment_two.astype(jnp.bfloat16)[None]  27.9 us
    dot_general x1, matrix products, local(): grad = jnp.dot(d_pre_t, centered, preferred_element_type=jnp.float32)  14.7 us
    dot_general x1, matrix products, local(): lax.dot_general(latent_t, decoder, (((0,), (0,)), ((), ())), preferred_el...  7.04 us
    dot_general x1, matrix products, local(): lax.dot_general(weight_in, centered, (((1,), (1,)), ((), ())), preferred_...  5.77 us
    all_gather x1, waiting for transfers between devices, local(): gathered = lax.all_gather(half_rows, 'seed', axis=0, tiled=True)  5.33 us
    reduce_sum x1, other arithmetic, local(): jnp.sum(jnp.square(decoder.astype(jnp.float32)), axis=1) + 1e-06  5.08 us
  transfers between devices with their start and end apart: 9, of which 9 were waited for; matrix products, arithmetic and copies ran while one was open for 3% of the time, Pallas kernels for 0%

profile of v1, /device:TPU:0, one launch (start us, length us, event | category | flops | bytes accessed | tf_op | source)
XLA Modules:
  0.0 236.6 jit_solution(8966899415361152966)
XLA Ops:
  7.2 0.0 copy-start
  7.2 0.0 copy-start.2
  7.2 0.0 all-gather.2.cloned.1.call-start
  7.2 3.0 %collective-permute-start = (bf16[128,256]{1,0:T(8,128)(2,1)}, bf16[128,256]{1,0:T(8,128)(2,1)S(1)}, u32[]{:S(2)}, u32[]{:S(2)}) collective-permute-start(bf16[128,256]{1,0:T(8,128)(2,1)} %param.9), channel_id=1, source_target_pairs={{0,2},{2,4},{4,6},{6,8},{8,10},{10,12},{12,14},{14,0},{1,3},{3,5},... | collective-permute-start | bytes 196616 | tf_op jit(solution)/shard_map/ppermute | solution.py:29
  10.2 5.5 %collective-permute-done = bf16[128,256]{1,0:T(8,128)(2,1)S(1)} collective-permute-done((bf16[128,256]{1,0:T(8,128)(2,1)}, bf16[128,256]{1,0:T(8,128)(2,1)S(1)}, u32[]{:S(2)}, u32[]{:S(2)}) %collective-permute-start) | collective-permute-done | bytes 65568 | tf_op jit(solution)/shard_map/ppermute | solution.py:29
  15.7 0.0 collective-permute-start.1
  15.7 7.0 %collective-permute-done.1 = bf16[128,256]{1,0:T(8,128)(2,1)S(1)} collective-permute-done((bf16[128,256]{1,0:T(8,128)(2,1)S(1)}, bf16[128,256]{1,0:T(8,128)(2,1)S(1)}, u32[]{:S(2)}, u32[]{:S(2)}) %collective-permute-start.1) | collective-permute-done | bytes 65568 | tf_op jit(solution)/shard_map/ppermute | solution.py:29
  22.7 0.0 collective-permute-start.2
  22.7 7.0 %collective-permute-done.2 = bf16[128,256]{1,0:T(8,128)(2,1)S(1)} collective-permute-done((bf16[128,256]{1,0:T(8,128)(2,1)S(1)}, bf16[128,256]{1,0:T(8,128)(2,1)S(1)}, u32[]{:S(2)}, u32[]{:S(2)}) %collective-permute-start.2) | collective-permute-done | bytes 65568 | tf_op jit(solution)/shard_map/ppermute | solution.py:29
  29.6 0.0 collective-permute-start.3
  29.6 7.0 %collective-permute-done.3 = bf16[128,256]{1,0:T(8,128)(2,1)S(1)} collective-permute-done((bf16[128,256]{1,0:T(8,128)(2,1)S(1)}, bf16[128,256]{1,0:T(8,128)(2,1)S(1)}, u32[]{:S(2)}, u32[]{:S(2)}) %collective-permute-start.3) | collective-permute-done | bytes 65568 | tf_op jit(solution)/shard_map/ppermute | solution.py:29
  36.6 0.0 collective-permute-start.4
  36.6 7.4 %collective-permute-done.4 = bf16[128,256]{1,0:T(8,128)(2,1)S(1)} collective-permute-done((bf16[128,256]{1,0:T(8,128)(2,1)S(1)}, bf16[128,256]{1,0:T(8,128)(2,1)S(1)}, u32[]{:S(2)}, u32[]{:S(2)}) %collective-permute-start.4) | collective-permute-done | bytes 65568 | tf_op jit(solution)/shard_map/ppermute | solution.py:29
  44.0 0.0 collective-permute-start.5
  44.0 7.0 %collective-permute-done.5 = bf16[128,256]{1,0:T(8,128)(2,1)S(1)} collective-permute-done((bf16[128,256]{1,0:T(8,128)(2,1)S(1)}, bf16[128,256]{1,0:T(8,128)(2,1)S(1)}, u32[]{:S(2)}, u32[]{:S(2)}) %collective-permute-start.5) | collective-permute-done | bytes 65568 | tf_op jit(solution)/shard_map/ppermute | solution.py:29
  51.0 0.0 collective-permute-start.6
  51.0 7.0 %collective-permute-done.6 = bf16[128,256]{1,0:T(8,128)(2,1)S(1)} collective-permute-done((bf16[128,256]{1,0:T(8,128)(2,1)S(1)}, bf16[128,256]{1,0:T(8,128)(2,1)S(1)}, u32[]{:S(2)}, u32[]{:S(2)}) %collective-permute-start.6) | collective-permute-done | bytes 65568 | tf_op jit(solution)/shard_map/ppermute | solution.py:29
  58.0 0.8 constant_dynamic-update-slice_fusion.8
  59.0 0.8 constant_dynamic-update-slice_fusion
  59.8 0.8 constant_dynamic-slice_fusion
  60.6 0.0 all-gather.2.cloned.1.call-update
  60.7 0.0 all-reduce.2.cloned.1.call-start
  60.7 0.7 compare_select_fusion
  61.4 0.7 compare_and_fusion
  62.1 5.3 %all-gather.2.cloned.1.call-done = bf16[256,2048]{1,0:T(8,128)(2,1)} async-done(((bf16[128,2048]{1,0:T(8,128)(2,1)}), bf16[256,2048]{1,0:T(8,128)(2,1)}) %all-gather.2.cloned.1.call-update) | async-done | bytes 1048592 | tf_op jit(solution)/shard_map/all_gather | solution.py:33
  67.4 3.7 %gather_fusion = bf16[256,2048]{1,0:T(8,128)(2,1)S(1)} fusion(bf16[256,2048]{1,0:T(8,128)(2,1)} %all-gather.2.cloned.1.call-done, s32[1024]{0:T(1024)S(1)} %pad_clamp_fusion), kind=kCustom, calls=%fused_computation | custom fusion | bytes 2098176 | tf_op jit(solution)/shard_map/jit(_take)/gather | solution.py:35
  71.2 0.0 copy-done
  71.2 0.0 copy-done.2
  71.2 5.8 %fusion.27 = f32[256,2048]{1,0:T(8,128)S(1)} fusion(bf16[1,2048,2048]{2,1,0:T(8,128)(2,1)} %param.12, f32[2048]{0:T(1024)S(1)} %bitcast.64, f32[2048]{0:T(1024)S(1)} %bitcast.59, bf16[256,2048]{1,0:T(8,128)(2,1)S(1)} %gather_fusion, pred[256]{0:T(512)(128)(4,1)S(1)} %compare_and_fusion), kind=kOutput, calls=%fused_computation.27 | convolution fusion | flops 2150105088 | bytes 11550976 | tf_op jit(solution)/shard_map/dot_general | solution.py:41
  77.0 0.0 copy-start.1
  77.0 7.0 %fusion.10 = f32[256,2048]{1,0:T(8,128)} fusion(bf16[1,2048,2048]{2,1,0:T(8,128)(2,1)} %param.14, f32[256,2048]{1,0:T(8,128)S(1)} %fusion.27), kind=kOutput, calls=%fused_computation.16 | convolution fusion | flops 2148532224 | bytes 12582912 | tf_op jit(solution)/shard_map/dot_general | solution.py:46
  84.0 0.0 all-reduce.2.cloned.1.call-update
  84.0 0.0 copy-done.1
  84.1 5.1 %multiply_reduce_fusion = f32[2048]{0:T(1024)S(1)} fusion(bf16[1,2048,2048]{2,1,0:T(8,128)(2,1)} %param.14), kind=kLoop, calls=%fused_computation.9 | loop fusion | flops 12580864 | bytes 8396800 | tf_op jit(solution)/shard_map/reduce_sum | solution.py:54
  89.2 98.0 %all-reduce.2.cloned.1.call-done = f32[256,2048]{1,0:T(8,128)} async-done(((f32[256,2048]{1,0:T(8,128)}), f32[256,2048]{1,0:T(8,128)}) %all-reduce.2.cloned.1.call-update) | async-done | bytes 2097168 | tf_op jit(solution)/shard_map/psum | solution.py:49
  187.2 14.7 %fusion.34 = f32[2048,2048]{1,0:T(8,128)} fusion(bf16[1,2048,2048]{2,1,0:T(8,128)(2,1)} %param.14, f32[256,2048]{1,0:T(8,128)S(1)} %fusion.27, f32[256,2048]{1,0:T(8,128)} %all-reduce.2.cloned.1.call-done, f32[2048]{0:T(1024)S(1)} %sqrt_multiply_fusion, f32[2048]{0:T(1024)S(1)} %bitcast.61, f32[2048]{0:T(1024)S(1)} %bitcast.60, ...), kind=kOutput, calls=%fused_computation.29 | convolution fusion | flops 4303355904 | bytes 30433536 | tf_op jit(solution)/shard_map/dot_general | solution.py:59
  201.9 27.9 %fusion.6 = (bf16[1,2048,2048]{2,1,0:T(8,128)(2,1)}, bf16[1,2048,2048]{2,1,0:T(8,128)(2,1)}, bf16[1,2048,2048]{2,1,0:T(8,128)(2,1)}) fusion(f32[2048,2048]{1,0:T(8,128)} %fusion.34, bf16[1,2048,2048]{2,1,0:T(8,128)(2,1)} %param.17, bf16[1,2048,2048]{2,1,0:T(8,128)(2,1)} %param.16, bf16[1,2048,2048]{2,1,0:T(8,128)(2,1)} %param.12), kind=kLoop, calls=%fused_computation.12 | loop fusion | flops 88080384 | bytes 67108864 | tf_op jit(solution)/shard_map/broadcast_in_dim | solution.py:68
  (17 shorter events, 0.1 us)
Async XLA Ops:
  7.2 64.0 %copy-start = (f32[1,2048]{1,0:T(1,128)S(1)}, f32[1,2048]{1,0:T(1,128)}, u32[]{:S(2)}) copy-start(f32[1,2048]{1,0:T(1,128)} %param.15) | copy-start | bytes 24580
  7.2 64.0 %copy-start.2 = (f32[1,2048]{1,0:T(1,128)S(1)}, f32[1,2048]{1,0:T(1,128)}, u32[]{:S(2)}) copy-start(f32[1,2048]{1,0:T(1,128)} %param.13) | copy-start | bytes 24580
  7.2 60.2 %all-gather.2.cloned.1.call-start = ((), (), s32[]{:S(2)}) async-start(), calls=%async_computation | async-start | bytes 1572864 | tf_op jit(solution)/shard_map/all_gather | solution.py:33
  7.2 8.5 %collective-permute-start = (bf16[128,256]{1,0:T(8,128)(2,1)}, bf16[128,256]{1,0:T(8,128)(2,1)S(1)}, u32[]{:S(2)}, u32[]{:S(2)}) collective-permute-start(bf16[128,256]{1,0:T(8,128)(2,1)} %param.9), channel_id=1, source_target_pairs={{0,2},{2,4},{4,6},{6,8},{8,10},{10,12},{12,14},{14,0},{1,3},{3,5},... | collective-permute-start | bytes 196616 | tf_op jit(solution)/shard_map/ppermute | solution.py:29
  15.7 7.0 %collective-permute-start.1 = (bf16[128,256]{1,0:T(8,128)(2,1)S(1)}, bf16[128,256]{1,0:T(8,128)(2,1)S(1)}, u32[]{:S(2)}, u32[]{:S(2)}) collective-permute-start(bf16[128,256]{1,0:T(8,128)(2,1)S(1)} %collective-permute-done), channel_id=1, source_target_pairs={{0,2},{2,4},{4,6},{6,8},{8,10},{10,12},{12,14},{14,0},{1,3},{3,5},... | collective-permute-start | bytes 196616 | tf_op jit(solution)/shard_map/ppermute | solution.py:29
  22.7 7.0 %collective-permute-start.2 = (bf16[128,256]{1,0:T(8,128)(2,1)S(1)}, bf16[128,256]{1,0:T(8,128)(2,1)S(1)}, u32[]{:S(2)}, u32[]{:S(2)}) collective-permute-start(bf16[128,256]{1,0:T(8,128)(2,1)S(1)} %collective-permute-done.1), channel_id=1, source_target_pairs={{0,2},{2,4},{4,6},{6,8},{8,10},{10,12},{12,14},{14,0},{1,3},{3,5},... | collective-permute-start | bytes 196616 | tf_op jit(solution)/shard_map/ppermute | solution.py:29
  29.6 7.0 %collective-permute-start.3 = (bf16[128,256]{1,0:T(8,128)(2,1)S(1)}, bf16[128,256]{1,0:T(8,128)(2,1)S(1)}, u32[]{:S(2)}, u32[]{:S(2)}) collective-permute-start(bf16[128,256]{1,0:T(8,128)(2,1)S(1)} %collective-permute-done.2), channel_id=1, source_target_pairs={{0,2},{2,4},{4,6},{6,8},{8,10},{10,12},{12,14},{14,0},{1,3},{3,5},... | collective-permute-start | bytes 196616 | tf_op jit(solution)/shard_map/ppermute | solution.py:29
  36.6 7.4 %collective-permute-start.4 = (bf16[128,256]{1,0:T(8,128)(2,1)S(1)}, bf16[128,256]{1,0:T(8,128)(2,1)S(1)}, u32[]{:S(2)}, u32[]{:S(2)}) collective-permute-start(bf16[128,256]{1,0:T(8,128)(2,1)S(1)} %collective-permute-done.3), channel_id=1, source_target_pairs={{0,2},{2,4},{4,6},{6,8},{8,10},{10,12},{12,14},{14,0},{1,3},{3,5},... | collective-permute-start | bytes 196616 | tf_op jit(solution)/shard_map/ppermute | solution.py:29
  44.0 7.0 %collective-permute-start.5 = (bf16[128,256]{1,0:T(8,128)(2,1)S(1)}, bf16[128,256]{1,0:T(8,128)(2,1)S(1)}, u32[]{:S(2)}, u32[]{:S(2)}) collective-permute-start(bf16[128,256]{1,0:T(8,128)(2,1)S(1)} %collective-permute-done.4), channel_id=1, source_target_pairs={{0,2},{2,4},{4,6},{6,8},{8,10},{10,12},{12,14},{14,0},{1,3},{3,5},... | collective-permute-start | bytes 196616 | tf_op jit(solution)/shard_map/ppermute | solution.py:29
  51.0 7.0 %collective-permute-start.6 = (bf16[128,256]{1,0:T(8,128)(2,1)S(1)}, bf16[128,256]{1,0:T(8,128)(2,1)S(1)}, u32[]{:S(2)}, u32[]{:S(2)}) collective-permute-start(bf16[128,256]{1,0:T(8,128)(2,1)S(1)} %collective-permute-done.5), channel_id=1, source_target_pairs={{0,2},{2,4},{4,6},{6,8},{8,10},{10,12},{12,14},{14,0},{1,3},{3,5},... | collective-permute-start | bytes 196616 | tf_op jit(solution)/shard_map/ppermute | solution.py:29
  60.7 126.5 %all-reduce.2.cloned.1.call-start = ((), (), s32[]{:S(2)}) async-start(), calls=%async_computation.1 | async-start | bytes 4194304 | tf_op jit(solution)/shard_map/psum | solution.py:49
  77.0 7.1 %copy-start.1 = (s32[1,2048]{1,0:T(1,128)S(1)}, s32[1,2048]{1,0:T(1,128)}, u32[]{:S(2)}) copy-start(s32[1,2048]{1,0:T(1,128)} %param.11) | copy-start | bytes 24580
Sparse Core Ops, SparseCore 0:
  60.8 6.5 all-gather.1
  84.2 103.0 all-reduce.1
